TPU v7x, 256 devices: a whole 4x4x8 slice. The times are simulated.
256 devices in a mesh: grp: 4 (over x_lo, core), gx: 16 (over z, x_hi), gy: 4 (over y).
Axes of the slice: x: 4 (x_hi: 2, x_lo: 2; x = x_hi * 2 + x_lo), y: 4, z: 8, core: 2. Of those that a mesh axis runs over, the one named last changes fastest.
Arguments:
- conc: float32 [4, 32, 1024, 1024], P('grp', None, 'gx', 'gy'), may hold values from 0 to 1
- velocity: bfloat16 [3, 4, 32, 1024, 1024], P(None, 'grp', None, 'gx', 'gy'), may hold values from -0.119628906 to 0.119628906
- porosity: bfloat16 [4, 32, 1024, 1024], P('grp', None, 'gx', 'gy'), may hold values from 0.099609375 to 0.3984375
- saturation: bfloat16 [4, 32, 1024, 1024], P('grp', None, 'gx', 'gy'), may hold values from 0.29882812 to 1
- layer_counts: int32 [8], replicated, may hold values from 1 to 24, 96 in all
- electrodes: int32 [4, 2], replicated, may hold values from 0 to 2097151
- init_potential: float32 [4, 8, 512, 512], P(None, None, 'gx', 'gy'), may hold values from -6 to 6
Outputs:
- conc_next: float32 [4, 32, 1024, 1024], P('grp', None, 'gx', 'gy')
- conductivity: float32 [8, 512, 512], P(None, 'gx', 'gy')
- potential: float32 [4, 8, 512, 512], P('grp', None, 'gx', 'gy')
Inputs may be any that keep to these rules, and one draw needn't show every extreme that they name: layer_counts sums to 96; its largest entry is exactly 24.
All inputs are finite; a program needn't handle non-finite values.
Results may differ from a plain program's by a relative error of at most 0.0014.
Values may be sent and summed in bfloat16 or wider, within the bound.
No kernel may reach another device: no remote copies, remote signals or barrier semaphores. Data moves between devices by JAX's collectives and lax.ppermute only.
A program may use at most 128 MiB of HBM per device.

v0:
```python
import jax
import jax.numpy as jnp
from jax import lax
from jax.sharding import PartitionSpec as P

SWEEPS = 3
KAPPA = 0.06
OMEGA = 0.8
AMPLITUDE = 40.0
ARCHIE = 20.0


def with_halo(shard, sides, width):
    for axis, dim in sides:
        devices, length = (lax.axis_size(axis), shard.shape[dim])
        up = [(i, (i + 1) % devices) for i in range(devices - 1)]
        down = [(j, i) for i, j in up]
        last = lax.slice_in_dim(shard, length - width, length, axis=dim)
        initial = lax.slice_in_dim(shard, 0, width, axis=dim)
        before = lax.ppermute(last, axis, up)
        after = lax.ppermute(initial, axis, down)
        shard = jnp.concatenate([before, shard, after], axis=dim)
    return shard


def neighbours(padded, direction_index):
    leading = [slice(None)] * (padded.ndim - 3)
    middle = [slice(1, -1)] * 3
    below_slices = list(middle)
    below_slices[direction_index] = slice(0, -2)
    above_slices = list(middle)
    above_slices[direction_index] = slice(2, None)
    return (padded[tuple(leading + below_slices)], padded[tuple(leading + above_slices)])


def tendency(padded, speeds):
    center = padded[1:-1, 1:-1, 1:-1]
    running = -6.0 * KAPPA * center
    for direction_index in range(3):
        below_cells, above_cells = neighbours(padded, direction_index)
        speed_comp = speeds[direction_index]
        running = (
            running
            + KAPPA * (below_cells + above_cells)
            - (
                jnp.maximum(speed_comp, 0.0) * (center - below_cells)
                + jnp.minimum(speed_comp, 0.0) * (above_cells - center)
            )
        )
    return running


def section_halo(values):
    return with_halo(values, (("grp", 0), ("gx", 1), ("gy", 2)), 1)


def potential_halo(values):
    return with_halo(values, (("gx", 2), ("gy", 3)), 1)


def face_terms(cond_padded, center):
    faces = []
    diagonal = jnp.zeros_like(center)
    for direction_index in range(3):
        below_cells, above_cells = neighbours(cond_padded, direction_index)
        face_below = 0.5 * (center + below_cells)
        face_above = 0.5 * (center + above_cells)
        faces.append((face_below, face_above))
        diagonal = diagonal + face_below + face_above
    return (faces, diagonal)


def sweep_once(potential, faces, diagonal, source_terms, pot_wide):
    coupled = jnp.zeros_like(potential)
    for direction_index in range(3):
        below_cells, above_cells = neighbours(pot_wide, direction_index)
        coupled = (
            coupled
            + faces[direction_index][0] * below_cells
            + faces[direction_index][1] * above_cells
        )
    applied = diagonal * potential - coupled
    return potential + OMEGA * (source_terms - applied) / diagonal


def on_device(conc, velocity, porosity, saturation, layer_counts, electrodes, init_potential):
    group_index = lax.axis_index("grp")
    row_index = lax.axis_index("gx")
    column_index = lax.axis_index("gy")
    active = group_index < 3
    field = jnp.where(active, conc[0], 0.0)
    speeds = velocity[:, 0].astype(jnp.float32)
    layers, tile_x, tile_y = field.shape
    section_one = jnp.where(active, field + tendency(section_halo(field), speeds), 0.0)
    advanced = 0.5 * (field + section_one + tendency(section_halo(section_one), speeds))
    advanced = jnp.where(active, advanced, 0.0)
    poro = porosity[0].astype(jnp.float32)
    water = saturation[0].astype(jnp.float32)
    sigma = ARCHIE * jnp.exp(advanced) * poro * poro * water * water
    coarse_x = tile_x // 2
    coarse_y = tile_y // 2
    coarse = sigma.reshape(layers, coarse_x, 2, coarse_y, 2).sum(axis=(2, 4))
    ends = jnp.cumsum(layer_counts)
    starts = ends - layer_counts
    layer_ids = group_index * layers + jnp.arange(layers, dtype=jnp.int32)
    member = (
        (layer_ids[None, :] >= starts[:, None]) & (layer_ids[None, :] < ends[:, None]) & active
    ).astype(jnp.float32)
    weights = member / (4.0 * layer_counts.astype(jnp.float32))[:, None]
    resist_layers = layer_counts.shape[0]
    partial_cond = jnp.dot(
        weights, coarse.reshape(layers, coarse_x * coarse_y), precision=lax.Precision.HIGHEST
    ).reshape(resist_layers, coarse_x, coarse_y)
    conductivity = lax.psum(partial_cond, "grp")
    grid_x = coarse_x * lax.axis_size("gx")
    grid_y = coarse_y * lax.axis_size("gy")
    potential = lax.dynamic_slice_in_dim(init_potential, group_index, 1, 0)
    poles = lax.dynamic_slice_in_dim(electrodes, group_index, 1, 0)
    cond_padded = jnp.pad(
        with_halo(conductivity, (("gx", 1), ("gy", 2)), 1), ((1, 1), (0, 0), (0, 0))
    )
    faces, diagonal = face_terms(cond_padded, conductivity)
    flat_ids = (
        jnp.arange(resist_layers, dtype=jnp.int32)[:, None, None] * (grid_x * grid_y)
        + (row_index * coarse_x + jnp.arange(coarse_x, dtype=jnp.int32))[None, :, None] * grid_y
        + (column_index * coarse_y + jnp.arange(coarse_y, dtype=jnp.int32))[None, None, :]
    )
    source_terms = AMPLITUDE * (
        (flat_ids[None] == poles[:, 0, None, None, None]).astype(jnp.float32)
        - (flat_ids[None] == poles[:, 1, None, None, None]).astype(jnp.float32)
    )
    for sweep_index in range(SWEEPS):
        pot_wide = jnp.pad(potential_halo(potential), ((0, 0), (1, 1), (0, 0), (0, 0)))
        potential = sweep_once(potential, faces, diagonal, source_terms, pot_wide)
    return (advanced[None], conductivity, potential)


def solution(mesh):
    in_specs = (
        P("grp", None, "gx", "gy"),
        P(None, "grp", None, "gx", "gy"),
        P("grp", None, "gx", "gy"),
        P("grp", None, "gx", "gy"),
        P(),
        P(),
        P(None, None, "gx", "gy"),
    )
    out_specs = (P("grp", None, "gx", "gy"), P(None, "gx", "gy"), P("grp", None, "gx", "gy"))
    return jax.shard_map(
        on_device, mesh=mesh, in_specs=in_specs, out_specs=out_specs, check_vma=False
    )
```

profile of v0, /device:TPU:70, one launch (start us, length us, event | category | flops | bytes accessed | tf_op | source)
XLA Modules:
  0.0 272.3 jit_solution(4352050345593786454)
XLA Ops:
  7.2 1.8 broadcast_select_fusion
  9.0 1.9 collective-permute-start
  11.0 3.6 %collective-permute-start.1 = (f32[1,64,256]{2,1,0:T(8,128)S(1)}, f32[1,64,256]{2,1,0:T(8,128)S(1)}, u32[]{:S(2)}, u32[]{:S(2)}) collective-permute-start(f32[1,64,256]{2,1,0:T(8,128)S(1)} %get-tuple-element.28), channel_id=1, source_target_pairs={{64,0},{128,64},{192,128},{65,1},{129,65},{193,129},{66,2},{130,66... | collective-permute-start | bytes 196616 | tf_op jit(solution)/shard_map/ppermute | solution.py:21
  15.3 4.7 %collective-permute-start.16 = (f32[1,8,1,128]{3,1,2,0:T(8,128)S(1)}, f32[1,8,1,128]{3,1,2,0:T(8,128)S(1)}, u32[]{:S(2)}, u32[]{:S(2)}) collective-permute-start(f32[1,8,1,128]{3,1,2,0:T(8,128)S(1)} %get-tuple-element.44), channel_id=1, source_target_pairs={{0,4},{4,8},{8,12},{12,16},{16,20},{20,24},{24,28},{28,32},{32,36}... | collective-permute-start | bytes 12296 | tf_op jit(solution)/shard_map/ppermute | solution.py:20
  20.0 2.7 collective-permute-start.17
  22.7 1.8 fusion.129
  26.8 5.6 %collective-permute-start.2 = (f32[34,1,256]{2,1,0:T(1,128)S(1)}, f32[34,1,256]{2,1,0:T(1,128)S(1)}, u32[]{:S(2)}, u32[]{:S(2)}) collective-permute-start(f32[34,1,256]{2,1,0:T(1,128)S(1)} %get-tuple-element.23), channel_id=1, source_target_pairs={{0,4},{4,8},{8,12},{12,16},{16,20},{20,24},{24,28},{28,32},{32,36}... | collective-permute-start | bytes 104456 | tf_op jit(solution)/shard_map/ppermute | solution.py:20
  32.4 1.9 collective-permute-start.3
  34.4 6.2 %collective-permute-done.3 = f32[34,1,256]{2,1,0:T(1,128)S(1)} collective-permute-done((f32[34,1,256]{2,1,0:T(1,128)S(1)}, f32[34,1,256]{2,1,0:T(1,128)S(1)}, u32[]{:S(2)}, u32[]{:S(2)}) %collective-permute-start.3) | collective-permute-done | bytes 34848 | tf_op jit(solution)/shard_map/ppermute | solution.py:21
  40.9 1.8 fusion.118
  42.8 1.8 copy.29
  44.6 3.5 %collective-permute-start.4 = (f32[34,66,1]{1,2,0:T(1,128)S(1)}, f32[34,66,1]{1,2,0:T(1,128)S(1)}, u32[]{:S(2)}, u32[]{:S(2)}) collective-permute-start(f32[34,66,1]{1,2,0:T(1,128)S(1)} %copy.29), channel_id=1, source_target_pairs={{0,1},{1,2},{2,3},{4,5},{5,6},{6,7},{8,9},{9,10},{10,11},{12,13},{... | collective-permute-start | bytes 26936 | tf_op jit(solution)/shard_map/ppermute | solution.py:20
  50.5 5.5 %convert_element_type.50 = f32[3,1,32,64,256]{4,3,2,1,0:T(8,128)} convert(bf16[3,1,32,64,256]{4,3,2,1,0:T(8,128)(2,1)} %param.8) | non-fusion elementwise | flops 1572864 | bytes 9437184 | tf_op jit(solution)/shard_map/convert_element_type | solution.py:92
  59.1 14.5 %fusion.31 = f32[32,64,256]{2,1,0:T(8,128)S(1)} fusion(f32[32,64,256]{2,1,0:T(8,128)} %copy-done.1, f32[34,1,256]{2,1,0:T(1,128)S(1)} %collective-permute-done.3, f32[1,64,256]{2,1,0:T(8,128)S(1)} %collective-permute-done.1, f32[1,64,256]{2,1,0:T(8,128)S(1)} %collective-permute-done, f32[34,1,256]{2,1,0:T(1,128)S(1)} %collective-permute-done.2, ...), kind=kLoop, calls=%fused_computation.66 | loop fusion | flops 28311552 | bytes 10704417 | tf_op jit(solution)/shard_map/jit(_where)/select_n | solution.py:94
  73.6 1.9 collective-permute-start.6
  75.6 3.6 %collective-permute-start.7 = (f32[1,64,256]{2,1,0:T(8,128)S(1)}, f32[1,64,256]{2,1,0:T(8,128)S(1)}, u32[]{:S(2)}, u32[]{:S(2)}) collective-permute-start(f32[1,64,256]{2,1,0:T(8,128)S(1)} %get-tuple-element.26), channel_id=1, source_target_pairs={{64,0},{128,64},{192,128},{65,1},{129,65},{193,129},{66,2},{130,66... | collective-permute-start | bytes 196616 | tf_op jit(solution)/shard_map/ppermute | solution.py:21
  81.2 4.8 %collective-permute-start.8 = (f32[34,1,256]{2,1,0:T(1,128)S(1)}, f32[34,1,256]{2,1,0:T(1,128)S(1)}, u32[]{:S(2)}, u32[]{:S(2)}) collective-permute-start(f32[34,1,256]{2,1,0:T(1,128)S(1)} %get-tuple-element.21), channel_id=1, source_target_pairs={{0,4},{4,8},{8,12},{12,16},{16,20},{20,24},{24,28},{28,32},{32,36}... | collective-permute-start | bytes 104456 | tf_op jit(solution)/shard_map/ppermute | solution.py:20
  86.0 2.5 collective-permute-start.9
  89.1 6.3 %collective-permute-done.9 = f32[34,1,256]{2,1,0:T(1,128)S(1)} collective-permute-done((f32[34,1,256]{2,1,0:T(1,128)S(1)}, f32[34,1,256]{2,1,0:T(1,128)S(1)}, u32[]{:S(2)}, u32[]{:S(2)}) %collective-permute-start.9) | collective-permute-done | bytes 34848 | tf_op jit(solution)/shard_map/ppermute | solution.py:21
  95.7 1.8 fusion.117
  97.6 1.7 copy.33
  99.3 4.6 %collective-permute-start.10 = (f32[34,66,1]{1,2,0:T(1,128)S(1)}, f32[34,66,1]{1,2,0:T(1,128)S(1)}, u32[]{:S(2)}, u32[]{:S(2)}) collective-permute-start(f32[34,66,1]{1,2,0:T(1,128)S(1)} %copy.33), channel_id=1, source_target_pairs={{0,1},{1,2},{2,3},{4,5},{5,6},{6,7},{8,9},{9,10},{10,11},{12,13},{... | collective-permute-start | bytes 26936 | tf_op jit(solution)/shard_map/ppermute | solution.py:20
  103.9 1.7 copy.35
  108.7 2.6 collective-permute-done.11
  112.8 11.8 %multiply_multiply_fusion = (f32[32,64,256]{2,1,0:T(8,128)}, f32[32,64,256]{2,1,0:T(8,128)}) fusion(bf16[1,32,64,256]{3,2,1,0:T(8,128)(2,1)} %param.10, bf16[1,32,64,256]{3,2,1,0:T(8,128)(2,1)} %param.9, f32[32,64,256]{2,1,0:T(8,128)S(1)} %fusion.31, f32[3,1,32,64,256]{4,3,2,1,0:T(8,128)} %convert_element_type.50, f32[34,66,1]{2,1,0:T(8,128)} %copy.36, ...), kind=kLoop, calls=%fused_computation | loop fusion | flops 33554432 | bytes 16996896 | tf_op jit(solution)/shard_map/mul | solution.py:99
  124.7 6.4 %copy.37 = f32[32,64,256]{0,2,1:T(8,128)} copy(f32[32,64,256]{2,1,0:T(8,128)} %get-tuple-element.15) | data formatting | bytes 4194304 | tf_op jit(solution)/shard_map/mul | solution.py:99
  131.0 9.5 %reduce_sum.9 = f32[32,32,128]{0,2,1:T(8,128)S(1)} reduce(f32[32,32,2,128,2]{0,4,3,2,1:T(2,128)} %bitcast.106, f32[]{:T(128)} %constant.8.clone.1), dimensions={2,4}, to_apply=%region_1.2 | reduce | flops 393216 | bytes 2621444 | tf_op jit(solution)/shard_map/reduce_sum | solution.py:102
  141.2 1.7 fusion.49
  143.0 40.0 %all-reduce.6.cloned.1.call-done = f32[8,32,128]{2,0,1:T(8,128)} async-done(((f32[8,32,128]{2,0,1:T(8,128)}), f32[8,32,128]{2,0,1:T(8,128)}) %all-reduce.6.cloned.1.call-update) | async-done | bytes 131088 | tf_op jit(solution)/shard_map/psum | solution.py:114
  183.8 4.1 %collective-permute-start.12 = (f32[8,1,128]{2,0,1:T(8,128)S(1)}, f32[8,1,128]{2,0,1:T(8,128)S(1)}, u32[]{:S(2)}, u32[]{:S(2)}) collective-permute-start(f32[8,1,128]{2,0,1:T(8,128)S(1)} %get-tuple-element.42), channel_id=1, source_target_pairs={{0,4},{4,8},{8,12},{12,16},{16,20},{20,24},{24,28},{28,32},{32,36}... | collective-permute-start | bytes 12296 | tf_op jit(solution)/shard_map/ppermute | solution.py:20
  188.0 3.4 %collective-permute-start.18 = (f32[1,8,34,1]{3,1,2,0:T(8,128)S(1)}, f32[1,8,34,1]{3,1,2,0:T(8,128)S(1)}, u32[]{:S(2)}, u32[]{:S(2)}) collective-permute-start(f32[1,8,34,1]{3,1,2,0:T(8,128)S(1)} %get-tuple-element.35), channel_id=1, source_target_pairs={{0,1},{1,2},{2,3},{4,5},{5,6},{6,7},{8,9},{9,10},{10,11},{12,13},{... | collective-permute-start | bytes 3272 | tf_op jit(solution)/shard_map/ppermute | solution.py:20
  192.7 3.2 %collective-permute-start.13 = (f32[8,1,128]{2,0,1:T(8,128)S(1)}, f32[8,1,128]{2,0,1:T(8,128)S(1)}, u32[]{:S(2)}, u32[]{:S(2)}) collective-permute-start(f32[8,1,128]{2,0,1:T(8,128)S(1)} %get-tuple-element.41), channel_id=1, source_target_pairs={{4,0},{8,4},{12,8},{16,12},{20,16},{24,20},{28,24},{32,28},{36,32}... | collective-permute-start | bytes 12296 | tf_op jit(solution)/shard_map/ppermute | solution.py:21
  196.9 3.7 %collective-permute-done.13 = f32[8,1,128]{2,0,1:T(8,128)S(1)} collective-permute-done((f32[8,1,128]{2,0,1:T(8,128)S(1)}, f32[8,1,128]{2,0,1:T(8,128)S(1)}, u32[]{:S(2)}, u32[]{:S(2)}) %collective-permute-start.13) | collective-permute-done | bytes 4128 | tf_op jit(solution)/shard_map/ppermute | solution.py:21
  200.7 4.6 %collective-permute-start.14 = (f32[8,34,1]{2,0,1:T(8,128)S(1)}, f32[8,34,1]{2,0,1:T(8,128)S(1)}, u32[]{:S(2)}, u32[]{:S(2)}) collective-permute-start(f32[8,34,1]{2,0,1:T(8,128)S(1)} %get-tuple-element.33), channel_id=1, source_target_pairs={{0,1},{1,2},{2,3},{4,5},{5,6},{6,7},{8,9},{9,10},{10,11},{12,13},{... | collective-permute-start | bytes 3272 | tf_op jit(solution)/shard_map/ppermute | solution.py:20
  207.8 4.4 %collective-permute-done.15 = f32[8,34,1]{2,0,1:T(8,128)S(1)} collective-permute-done((f32[8,34,1]{2,0,1:T(8,128)S(1)}, f32[8,34,1]{2,0,1:T(8,128)S(1)}, u32[]{:S(2)}, u32[]{:S(2)}) %collective-permute-start.15) | collective-permute-done | bytes 1120 | tf_op jit(solution)/shard_map/ppermute | solution.py:21
  212.5 1.8 fusion.86
  214.3 3.3 %collective-permute-start.20 = (f32[1,8,1,128]{3,1,2,0:T(8,128)S(1)}, f32[1,8,1,128]{3,1,2,0:T(8,128)S(1)}, u32[]{:S(2)}, u32[]{:S(2)}) collective-permute-start(f32[1,8,1,128]{3,1,2,0:T(8,128)S(1)} %get-tuple-element.39), channel_id=1, source_target_pairs={{0,4},{4,8},{8,12},{12,16},{16,20},{20,24},{24,28},{28,32},{32,36}... | collective-permute-start | bytes 12296 | tf_op jit(solution)/shard_map/ppermute | solution.py:20
  217.7 4.0 %collective-permute-start.21 = (f32[1,8,1,128]{3,1,2,0:T(8,128)S(1)}, f32[1,8,1,128]{3,1,2,0:T(8,128)S(1)}, u32[]{:S(2)}, u32[]{:S(2)}) collective-permute-start(f32[1,8,1,128]{3,1,2,0:T(8,128)S(1)} %get-tuple-element.40), channel_id=1, source_target_pairs={{4,0},{8,4},{12,8},{16,12},{20,16},{24,20},{28,24},{32,28},{36,32}... | collective-permute-start | bytes 12296 | tf_op jit(solution)/shard_map/ppermute | solution.py:21
  221.7 5.0 %collective-permute-done.21 = f32[1,8,1,128]{3,1,2,0:T(8,128)S(1)} collective-permute-done((f32[1,8,1,128]{3,1,2,0:T(8,128)S(1)}, f32[1,8,1,128]{3,1,2,0:T(8,128)S(1)}, u32[]{:S(2)}, u32[]{:S(2)}) %collective-permute-start.21) | collective-permute-done | bytes 4128 | tf_op jit(solution)/shard_map/ppermute | solution.py:21
  226.8 3.4 %collective-permute-start.22 = (f32[1,8,34,1]{3,1,2,0:T(8,128)S(1)}, f32[1,8,34,1]{3,1,2,0:T(8,128)S(1)}, u32[]{:S(2)}, u32[]{:S(2)}) collective-permute-start(f32[1,8,34,1]{3,1,2,0:T(8,128)S(1)} %get-tuple-element.31), channel_id=1, source_target_pairs={{0,1},{1,2},{2,3},{4,5},{5,6},{6,7},{8,9},{9,10},{10,11},{12,13},{... | collective-permute-start | bytes 3272 | tf_op jit(solution)/shard_map/ppermute | solution.py:20
  232.8 4.4 %collective-permute-done.23 = f32[1,8,34,1]{3,1,2,0:T(8,128)S(1)} collective-permute-done((f32[1,8,34,1]{3,1,2,0:T(8,128)S(1)}, f32[1,8,34,1]{3,1,2,0:T(8,128)S(1)}, u32[]{:S(2)}, u32[]{:S(2)}) %collective-permute-start.23) | collective-permute-done | bytes 1120 | tf_op jit(solution)/shard_map/ppermute | solution.py:21
  237.4 1.8 fusion.72
  239.2 5.4 %collective-permute-start.24 = (f32[1,8,1,128]{3,1,2,0:T(8,128)S(1)}, f32[1,8,1,128]{3,1,2,0:T(8,128)S(1)}, u32[]{:S(2)}, u32[]{:S(2)}) collective-permute-start(f32[1,8,1,128]{3,1,2,0:T(8,128)S(1)} %get-tuple-element.37), channel_id=1, source_target_pairs={{0,4},{4,8},{8,12},{12,16},{16,20},{20,24},{24,28},{28,32},{32,36}... | collective-permute-start | bytes 12296 | tf_op jit(solution)/shard_map/ppermute | solution.py:20
  244.7 1.9 collective-permute-start.25
  246.6 6.0 %collective-permute-done.25 = f32[1,8,1,128]{3,1,2,0:T(8,128)S(1)} collective-permute-done((f32[1,8,1,128]{3,1,2,0:T(8,128)S(1)}, f32[1,8,1,128]{3,1,2,0:T(8,128)S(1)}, u32[]{:S(2)}, u32[]{:S(2)}) %collective-permute-start.25) | collective-permute-done | bytes 4128 | tf_op jit(solution)/shard_map/ppermute | solution.py:21
  252.7 3.1 %collective-permute-start.26 = (f32[1,8,34,1]{3,1,2,0:T(8,128)S(1)}, f32[1,8,34,1]{3,1,2,0:T(8,128)S(1)}, u32[]{:S(2)}, u32[]{:S(2)}) collective-permute-start(f32[1,8,34,1]{3,1,2,0:T(8,128)S(1)} %get-tuple-element.29), channel_id=1, source_target_pairs={{0,1},{1,2},{2,3},{4,5},{5,6},{6,7},{8,9},{9,10},{10,11},{12,13},{... | collective-permute-start | bytes 3272 | tf_op jit(solution)/shard_map/ppermute | solution.py:20
  258.4 4.4 %collective-permute-done.27 = f32[1,8,34,1]{3,1,2,0:T(8,128)S(1)} collective-permute-done((f32[1,8,34,1]{3,1,2,0:T(8,128)S(1)}, f32[1,8,34,1]{3,1,2,0:T(8,128)S(1)}, u32[]{:S(2)}, u32[]{:S(2)}) %collective-permute-start.27) | collective-permute-done | bytes 1120 | tf_op jit(solution)/shard_map/ppermute | solution.py:21
  263.0 1.8 fusion.58
  (91 shorter events, 29.7 us)
Async XLA Ops:
  7.2 7.5 %copy-start = (f32[4,8,32,128]{3,2,1,0:T(8,128)S(1)}, f32[4,8,32,128]{3,2,1,0:T(8,128)}, u32[]{:S(2)}) copy-start(f32[4,8,32,128]{3,2,1,0:T(8,128)} %param.13) | copy-start | bytes 1572868
  7.2 175.8 %all-reduce.6.cloned.1.call-start = ((), (), s32[]{:S(2)}) async-start(), calls=%async_computation | async-start | bytes 262144 | tf_op jit(solution)/shard_map/psum | solution.py:114
  9.0 17.7 %collective-permute-start = (f32[1,64,256]{2,1,0:T(8,128)S(1)}, f32[1,64,256]{2,1,0:T(8,128)S(1)}, u32[]{:S(2)}, u32[]{:S(2)}) collective-permute-start(f32[1,64,256]{2,1,0:T(8,128)S(1)} %get-tuple-element.27), channel_id=1, source_target_pairs={{0,64},{64,128},{128,192},{1,65},{65,129},{129,193},{2,66},{66,130... | collective-permute-start | bytes 196616 | tf_op jit(solution)/shard_map/ppermute | solution.py:20
  11.0 15.8 %collective-permute-start.1 = (f32[1,64,256]{2,1,0:T(8,128)S(1)}, f32[1,64,256]{2,1,0:T(8,128)S(1)}, u32[]{:S(2)}, u32[]{:S(2)}) collective-permute-start(f32[1,64,256]{2,1,0:T(8,128)S(1)} %get-tuple-element.28), channel_id=1, source_target_pairs={{64,0},{128,64},{192,128},{65,1},{129,65},{193,129},{66,2},{130,66... | collective-permute-start | bytes 196616 | tf_op jit(solution)/shard_map/ppermute | solution.py:21
  15.3 91.8 %collective-permute-start.16 = (f32[1,8,1,128]{3,1,2,0:T(8,128)S(1)}, f32[1,8,1,128]{3,1,2,0:T(8,128)S(1)}, u32[]{:S(2)}, u32[]{:S(2)}) collective-permute-start(f32[1,8,1,128]{3,1,2,0:T(8,128)S(1)} %get-tuple-element.44), channel_id=1, source_target_pairs={{0,4},{4,8},{8,12},{12,16},{16,20},{20,24},{24,28},{28,32},{32,36}... | collective-permute-start | bytes 12296 | tf_op jit(solution)/shard_map/ppermute | solution.py:20
  20.0 4.5 %copy-start.8 = (s32[8]{0:T(128)S(1)}, s32[8]{0:T(128)}, u32[]{:S(2)}) copy-start(s32[8]{0:T(128)} %param.11) | copy-start | bytes 100
  20.0 123.0 %collective-permute-start.17 = (f32[1,8,1,128]{3,1,2,0:T(8,128)}, f32[1,8,1,128]{3,1,2,0:T(8,128)S(1)}, u32[]{:S(2)}, u32[]{:S(2)}) collective-permute-start(f32[1,8,1,128]{3,1,2,0:T(8,128)} %get-tuple-element.43), channel_id=1, source_target_pairs={{4,0},{8,4},{12,8},{16,12},{20,16},{24,20},{28,24},{32,28},{36,32}... | collective-permute-start | bytes 12296 | tf_op jit(solution)/shard_map/ppermute | solution.py:21
  24.5 16.4 %copy-start.1 = (f32[32,64,256]{2,1,0:T(8,128)}, f32[32,64,256]{2,1,0:T(8,128)S(1)}, u32[]{:S(2)}) copy-start(f32[32,64,256]{2,1,0:T(8,128)S(1)} %fusion.129) | copy-start | bytes 6291460
  24.5 9.8 %copy-start.6 = (s32[4,2]{0,1:T(2,128)S(1)}, s32[4,2]{0,1:T(2,128)}, u32[]{:S(2)}) copy-start(s32[4,2]{0,1:T(2,128)} %param.12) | copy-start | bytes 100
  24.7 0.8 copy-start.7
  26.8 7.6 %collective-permute-start.2 = (f32[34,1,256]{2,1,0:T(1,128)S(1)}, f32[34,1,256]{2,1,0:T(1,128)S(1)}, u32[]{:S(2)}, u32[]{:S(2)}) collective-permute-start(f32[34,1,256]{2,1,0:T(1,128)S(1)} %get-tuple-element.23), channel_id=1, source_target_pairs={{0,4},{4,8},{8,12},{12,16},{16,20},{20,24},{24,28},{28,32},{32,36}... | collective-permute-start | bytes 104456 | tf_op jit(solution)/shard_map/ppermute | solution.py:20
  32.4 8.2 %collective-permute-start.3 = (f32[34,1,256]{2,1,0:T(1,128)S(1)}, f32[34,1,256]{2,1,0:T(1,128)S(1)}, u32[]{:S(2)}, u32[]{:S(2)}) collective-permute-start(f32[34,1,256]{2,1,0:T(1,128)S(1)} %get-tuple-element.24), channel_id=1, source_target_pairs={{4,0},{8,4},{12,8},{16,12},{20,16},{24,20},{28,24},{32,28},{36,32}... | collective-permute-start | bytes 104456 | tf_op jit(solution)/shard_map/ppermute | solution.py:21
  42.7 5.3 %copy-start.2 = (f32[34,66,1]{2,1,0:T(8,128)S(1)}, f32[34,66,1]{2,1,0:T(8,128)}, u32[]{:S(2)}) copy-start(f32[34,66,1]{2,1,0:T(8,128)} %get-tuple-element.19) | copy-start | bytes 26932
  44.6 11.3 %collective-permute-start.4 = (f32[34,66,1]{1,2,0:T(1,128)S(1)}, f32[34,66,1]{1,2,0:T(1,128)S(1)}, u32[]{:S(2)}, u32[]{:S(2)}) collective-permute-start(f32[34,66,1]{1,2,0:T(1,128)S(1)} %copy.29), channel_id=1, source_target_pairs={{0,1},{1,2},{2,3},{4,5},{5,6},{6,7},{8,9},{9,10},{10,11},{12,13},{... | collective-permute-start | bytes 26936 | tf_op jit(solution)/shard_map/ppermute | solution.py:20
  48.6 8.9 %collective-permute-start.5 = (f32[34,66,1]{1,2,0:T(1,128)S(1)}, f32[34,66,1]{1,2,0:T(1,128)S(1)}, u32[]{:S(2)}, u32[]{:S(2)}) collective-permute-start(f32[34,66,1]{1,2,0:T(1,128)S(1)} %copy.31), channel_id=1, source_target_pairs={{1,0},{2,1},{3,2},{5,4},{6,5},{7,6},{9,8},{10,9},{11,10},{13,12},{... | collective-permute-start | bytes 26936 | tf_op jit(solution)/shard_map/ppermute | solution.py:21
  73.6 6.1 %collective-permute-start.6 = (f32[1,64,256]{2,1,0:T(8,128)S(1)}, f32[1,64,256]{2,1,0:T(8,128)S(1)}, u32[]{:S(2)}, u32[]{:S(2)}) collective-permute-start(f32[1,64,256]{2,1,0:T(8,128)S(1)} %get-tuple-element.25), channel_id=1, source_target_pairs={{0,64},{64,128},{128,192},{1,65},{65,129},{129,193},{2,66},{66,130... | collective-permute-start | bytes 196616 | tf_op jit(solution)/shard_map/ppermute | solution.py:20
  75.6 5.5 %collective-permute-start.7 = (f32[1,64,256]{2,1,0:T(8,128)S(1)}, f32[1,64,256]{2,1,0:T(8,128)S(1)}, u32[]{:S(2)}, u32[]{:S(2)}) collective-permute-start(f32[1,64,256]{2,1,0:T(8,128)S(1)} %get-tuple-element.26), channel_id=1, source_target_pairs={{64,0},{128,64},{192,128},{65,1},{129,65},{193,129},{66,2},{130,66... | collective-permute-start | bytes 196616 | tf_op jit(solution)/shard_map/ppermute | solution.py:21
  81.2 8.0 %collective-permute-start.8 = (f32[34,1,256]{2,1,0:T(1,128)S(1)}, f32[34,1,256]{2,1,0:T(1,128)S(1)}, u32[]{:S(2)}, u32[]{:S(2)}) collective-permute-start(f32[34,1,256]{2,1,0:T(1,128)S(1)} %get-tuple-element.21), channel_id=1, source_target_pairs={{0,4},{4,8},{8,12},{12,16},{16,20},{20,24},{24,28},{28,32},{32,36}... | collective-permute-start | bytes 104456 | tf_op jit(solution)/shard_map/ppermute | solution.py:20
  86.0 9.4 %collective-permute-start.9 = (f32[34,1,256]{2,1,0:T(1,128)S(1)}, f32[34,1,256]{2,1,0:T(1,128)S(1)}, u32[]{:S(2)}, u32[]{:S(2)}) collective-permute-start(f32[34,1,256]{2,1,0:T(1,128)S(1)} %get-tuple-element.22), channel_id=1, source_target_pairs={{4,0},{8,4},{12,8},{16,12},{20,16},{24,20},{28,24},{32,28},{36,32}... | collective-permute-start | bytes 104456 | tf_op jit(solution)/shard_map/ppermute | solution.py:21
  99.3 7.8 %collective-permute-start.10 = (f32[34,66,1]{1,2,0:T(1,128)S(1)}, f32[34,66,1]{1,2,0:T(1,128)S(1)}, u32[]{:S(2)}, u32[]{:S(2)}) collective-permute-start(f32[34,66,1]{1,2,0:T(1,128)S(1)} %copy.33), channel_id=1, source_target_pairs={{0,1},{1,2},{2,3},{4,5},{5,6},{6,7},{8,9},{9,10},{10,11},{12,13},{... | collective-permute-start | bytes 26936 | tf_op jit(solution)/shard_map/ppermute | solution.py:20
  105.6 5.7 %collective-permute-start.11 = (f32[34,66,1]{1,2,0:T(1,128)S(1)}, f32[34,66,1]{1,2,0:T(1,128)S(1)}, u32[]{:S(2)}, u32[]{:S(2)}) collective-permute-start(f32[34,66,1]{1,2,0:T(1,128)S(1)} %copy.35), channel_id=1, source_target_pairs={{1,0},{2,1},{3,2},{5,4},{6,5},{7,6},{9,8},{10,9},{11,10},{13,12},{... | collective-permute-start | bytes 26936 | tf_op jit(solution)/shard_map/ppermute | solution.py:21
  141.2 71.3 %copy-start.4 = (s32[8,32]{0,1:T(8,128)S(1)}, s32[8,32]{0,1:T(8,128)}, u32[]{:S(2)}) copy-start(s32[8,32]{0,1:T(8,128)} %broadcast_add_fusion) | copy-start | bytes 3076
  141.2 71.4 %copy-start.5 = (s32[128]{0:T(128)S(1)}, s32[128]{0:T(128)}, u32[]{:S(2)}) copy-start(s32[128]{0:T(128)} %iota_add_fusion) | copy-start | bytes 1540
  183.0 29.5 %copy-start.3 = (f32[8,32,128]{2,0,1:T(8,128)S(1)}, f32[8,32,128]{2,0,1:T(8,128)}, u32[]{:S(2)}) copy-start(f32[8,32,128]{2,0,1:T(8,128)} %all-reduce.6.cloned.1.call-done) | copy-start | bytes 393220
  183.8 12.2 %collective-permute-start.12 = (f32[8,1,128]{2,0,1:T(8,128)S(1)}, f32[8,1,128]{2,0,1:T(8,128)S(1)}, u32[]{:S(2)}, u32[]{:S(2)}) collective-permute-start(f32[8,1,128]{2,0,1:T(8,128)S(1)} %get-tuple-element.42), channel_id=1, source_target_pairs={{0,4},{4,8},{8,12},{12,16},{16,20},{20,24},{24,28},{28,32},{32,36}... | collective-permute-start | bytes 12296 | tf_op jit(solution)/shard_map/ppermute | solution.py:20
  188.0 18.6 %collective-permute-start.18 = (f32[1,8,34,1]{3,1,2,0:T(8,128)S(1)}, f32[1,8,34,1]{3,1,2,0:T(8,128)S(1)}, u32[]{:S(2)}, u32[]{:S(2)}) collective-permute-start(f32[1,8,34,1]{3,1,2,0:T(8,128)S(1)} %get-tuple-element.35), channel_id=1, source_target_pairs={{0,1},{1,2},{2,3},{4,5},{5,6},{6,7},{8,9},{9,10},{10,11},{12,13},{... | collective-permute-start | bytes 3272 | tf_op jit(solution)/shard_map/ppermute | solution.py:20
  191.4 15.2 %collective-permute-start.19 = (f32[1,8,34,1]{3,1,2,0:T(8,128)S(1)}, f32[1,8,34,1]{3,1,2,0:T(8,128)S(1)}, u32[]{:S(2)}, u32[]{:S(2)}) collective-permute-start(f32[1,8,34,1]{3,1,2,0:T(8,128)S(1)} %get-tuple-element.36), channel_id=1, source_target_pairs={{1,0},{2,1},{3,2},{5,4},{6,5},{7,6},{9,8},{10,9},{11,10},{13,12},{... | collective-permute-start | bytes 3272 | tf_op jit(solution)/shard_map/ppermute | solution.py:21
  192.7 7.9 %collective-permute-start.13 = (f32[8,1,128]{2,0,1:T(8,128)S(1)}, f32[8,1,128]{2,0,1:T(8,128)S(1)}, u32[]{:S(2)}, u32[]{:S(2)}) collective-permute-start(f32[8,1,128]{2,0,1:T(8,128)S(1)} %get-tuple-element.41), channel_id=1, source_target_pairs={{4,0},{8,4},{12,8},{16,12},{20,16},{24,20},{28,24},{32,28},{36,32}... | collective-permute-start | bytes 12296 | tf_op jit(solution)/shard_map/ppermute | solution.py:21
  200.7 7.1 %collective-permute-start.14 = (f32[8,34,1]{2,0,1:T(8,128)S(1)}, f32[8,34,1]{2,0,1:T(8,128)S(1)}, u32[]{:S(2)}, u32[]{:S(2)}) collective-permute-start(f32[8,34,1]{2,0,1:T(8,128)S(1)} %get-tuple-element.33), channel_id=1, source_target_pairs={{0,1},{1,2},{2,3},{4,5},{5,6},{6,7},{8,9},{9,10},{10,11},{12,13},{... | collective-permute-start | bytes 3272 | tf_op jit(solution)/shard_map/ppermute | solution.py:20
  205.3 6.9 %collective-permute-start.15 = (f32[8,34,1]{2,0,1:T(8,128)S(1)}, f32[8,34,1]{2,0,1:T(8,128)S(1)}, u32[]{:S(2)}, u32[]{:S(2)}) collective-permute-start(f32[8,34,1]{2,0,1:T(8,128)S(1)} %get-tuple-element.34), channel_id=1, source_target_pairs={{1,0},{2,1},{3,2},{5,4},{6,5},{7,6},{9,8},{10,9},{11,10},{13,12},{... | collective-permute-start | bytes 3272 | tf_op jit(solution)/shard_map/ppermute | solution.py:21
  214.3 7.4 %collective-permute-start.20 = (f32[1,8,1,128]{3,1,2,0:T(8,128)S(1)}, f32[1,8,1,128]{3,1,2,0:T(8,128)S(1)}, u32[]{:S(2)}, u32[]{:S(2)}) collective-permute-start(f32[1,8,1,128]{3,1,2,0:T(8,128)S(1)} %get-tuple-element.39), channel_id=1, source_target_pairs={{0,4},{4,8},{8,12},{12,16},{16,20},{20,24},{24,28},{28,32},{32,36}... | collective-permute-start | bytes 12296 | tf_op jit(solution)/shard_map/ppermute | solution.py:20
  217.7 9.0 %collective-permute-start.21 = (f32[1,8,1,128]{3,1,2,0:T(8,128)S(1)}, f32[1,8,1,128]{3,1,2,0:T(8,128)S(1)}, u32[]{:S(2)}, u32[]{:S(2)}) collective-permute-start(f32[1,8,1,128]{3,1,2,0:T(8,128)S(1)} %get-tuple-element.40), channel_id=1, source_target_pairs={{4,0},{8,4},{12,8},{16,12},{20,16},{24,20},{28,24},{32,28},{36,32}... | collective-permute-start | bytes 12296 | tf_op jit(solution)/shard_map/ppermute | solution.py:21
  226.8 6.0 %collective-permute-start.22 = (f32[1,8,34,1]{3,1,2,0:T(8,128)S(1)}, f32[1,8,34,1]{3,1,2,0:T(8,128)S(1)}, u32[]{:S(2)}, u32[]{:S(2)}) collective-permute-start(f32[1,8,34,1]{3,1,2,0:T(8,128)S(1)} %get-tuple-element.31), channel_id=1, source_target_pairs={{0,1},{1,2},{2,3},{4,5},{5,6},{6,7},{8,9},{9,10},{10,11},{12,13},{... | collective-permute-start | bytes 3272 | tf_op jit(solution)/shard_map/ppermute | solution.py:20
  230.2 6.9 %collective-permute-start.23 = (f32[1,8,34,1]{3,1,2,0:T(8,128)S(1)}, f32[1,8,34,1]{3,1,2,0:T(8,128)S(1)}, u32[]{:S(2)}, u32[]{:S(2)}) collective-permute-start(f32[1,8,34,1]{3,1,2,0:T(8,128)S(1)} %get-tuple-element.32), channel_id=1, source_target_pairs={{1,0},{2,1},{3,2},{5,4},{6,5},{7,6},{9,8},{10,9},{11,10},{13,12},{... | collective-permute-start | bytes 3272 | tf_op jit(solution)/shard_map/ppermute | solution.py:21
  239.2 7.4 %collective-permute-start.24 = (f32[1,8,1,128]{3,1,2,0:T(8,128)S(1)}, f32[1,8,1,128]{3,1,2,0:T(8,128)S(1)}, u32[]{:S(2)}, u32[]{:S(2)}) collective-permute-start(f32[1,8,1,128]{3,1,2,0:T(8,128)S(1)} %get-tuple-element.37), channel_id=1, source_target_pairs={{0,4},{4,8},{8,12},{12,16},{16,20},{20,24},{24,28},{28,32},{32,36}... | collective-permute-start | bytes 12296 | tf_op jit(solution)/shard_map/ppermute | solution.py:20
  244.7 7.9 %collective-permute-start.25 = (f32[1,8,1,128]{3,1,2,0:T(8,128)S(1)}, f32[1,8,1,128]{3,1,2,0:T(8,128)S(1)}, u32[]{:S(2)}, u32[]{:S(2)}) collective-permute-start(f32[1,8,1,128]{3,1,2,0:T(8,128)S(1)} %get-tuple-element.38), channel_id=1, source_target_pairs={{4,0},{8,4},{12,8},{16,12},{20,16},{24,20},{28,24},{32,28},{36,32}... | collective-permute-start | bytes 12296 | tf_op jit(solution)/shard_map/ppermute | solution.py:21
  252.7 5.7 %collective-permute-start.26 = (f32[1,8,34,1]{3,1,2,0:T(8,128)S(1)}, f32[1,8,34,1]{3,1,2,0:T(8,128)S(1)}, u32[]{:S(2)}, u32[]{:S(2)}) collective-permute-start(f32[1,8,34,1]{3,1,2,0:T(8,128)S(1)} %get-tuple-element.29), channel_id=1, source_target_pairs={{0,1},{1,2},{2,3},{4,5},{5,6},{6,7},{8,9},{9,10},{10,11},{12,13},{... | collective-permute-start | bytes 3272 | tf_op jit(solution)/shard_map/ppermute | solution.py:20
  255.8 6.9 %collective-permute-start.27 = (f32[1,8,34,1]{3,1,2,0:T(8,128)S(1)}, f32[1,8,34,1]{3,1,2,0:T(8,128)S(1)}, u32[]{:S(2)}, u32[]{:S(2)}) collective-permute-start(f32[1,8,34,1]{3,1,2,0:T(8,128)S(1)} %get-tuple-element.30), channel_id=1, source_target_pairs={{1,0},{2,1},{3,2},{5,4},{6,5},{7,6},{9,8},{10,9},{11,10},{13,12},{... | collective-permute-start | bytes 3272 | tf_op jit(solution)/shard_map/ppermute | solution.py:21
Sparse Core Ops, SparseCore 0:
  143.0 39.9 all-reduce.5
where the time goes:
time: 274 us; the launch traced here: 272 us
  waiting for transfers between devices  87.1 us (32%)
  starting transfers between devices  85.8 us (31%)
  other arithmetic  55.4 us (20%)
  local copies, waits for them, and re-layouts  27.6 us (10%)
  between operations  14.6 us (5%)
    ppermute x14, starting transfers between devices, with_halo(): before = lax.ppermute(last, axis, up)  54.2 us
    ppermute x14, waiting for transfers between devices, with_halo(): after = lax.ppermute(initial, axis, down)  44.2 us
    psum x1, waiting for transfers between devices, on_device(): conductivity = lax.psum(partial_cond, 'grp')  40 us
    ppermute x14, starting transfers between devices, with_halo(): after = lax.ppermute(initial, axis, down)  31.6 us
    select_n x1, other arithmetic, on_device(): jnp.where(active, field + tendency(section_halo(field), speeds), 0.0)  14.5 us
    mul x1, other arithmetic, on_device(): sigma = ARCHIE * jnp.exp(advanced) * poro * poro * water * water  11.8 us
    reduce_sum x1, other arithmetic, on_device(): coarse = sigma.reshape(layers, coarse_x, 2, coarse_y, 2).sum(axis=(2, 4))  9.53 us
    mul x1, local copies, waits for them, and re-layouts, on_device(): sigma = ARCHIE * jnp.exp(advanced) * poro * poro * water * water  6.37 us
  transfers between devices with their start and end apart: 29, of which 14 were waited for; matrix products, arithmetic and copies ran while one was open for 28% of the time, Pallas kernels for 0%

commit v1 on v0

--- a/solution.py
+++ b/solution.py
@@ -1,3 +1,4 @@
+import functools
 import jax
 import jax.numpy as jnp
 from jax import lax
@@ -8,6 +9,14 @@
 OMEGA = 0.8
 AMPLITUDE = 40.0
 ARCHIE = 20.0
+
+
+def serve_the_stops_all(base_x, axis_name):
+    newest = lax.all_gather(base_x, axis_name)
+    return jnp.sum(newest, axis=0)
+
+
+store_shards = functools.partial(serve_the_stops_all, axis_name="grp")
 
 
 def with_halo(shard, sides, width):
@@ -111,7 +120,7 @@
     partial_cond = jnp.dot(
         weights, coarse.reshape(layers, coarse_x * coarse_y), precision=lax.Precision.HIGHEST
     ).reshape(resist_layers, coarse_x, coarse_y)
-    conductivity = lax.psum(partial_cond, "grp")
+    conductivity = store_shards(partial_cond)
     grid_x = coarse_x * lax.axis_size("gx")
     grid_y = coarse_y * lax.axis_size("gy")
     potential = lax.dynamic_slice_in_dim(init_potential, group_index, 1, 0)

time: 274 us -> 217 us (0.79)
  waiting for transfers between devices: 87.1 us -> 43.3 us
  between operations: 14.6 us -> 1.27 us
  blocking collectives: 0 us -> 6.51 us
  other arithmetic: 55.4 us -> 51.9 us
    psum x1 -> x0, waiting for transfers between devices: 40 us -> none  [on_device(): conductivity = lax.psum(partial_cond, 'grp')]
    all_gather x0 -> x1, blocking collectives: none -> 6.51 us  [serve_the_stops_all(): newest = lax.all_gather(base_x, axis_name)]
    ppermute x14, waiting for transfers between devices: 44.2 us -> 40.5 us  [with_halo(): after = lax.ppermute(initial, axis, down)]
    slice x11 -> x10, local copies, waits for them, and re-layouts: 5.82 us -> 5.73 us  [with_halo(): last = lax.slice_in_dim(shard, length - width, length, axis=dim)]
  transfers between devices with their start and end apart: 29 -> 28, of which waited for: 14 -> 13; matrix products, arithmetic and copies ran while one was open for 28% -> 18% of each run, Pallas kernels for 0% -> 0%
where the time goes in v1:
time: 217 us; the launch traced here: 213 us
  starting transfers between devices  84.4 us (39%)
  other arithmetic  51.9 us (24%)
  waiting for transfers between devices  43.3 us (20%)
  local copies, waits for them, and re-layouts  25.6 us (12%)
  blocking collectives  6.51 us (3%)
    ppermute x14, starting transfers between devices, with_halo(): before = lax.ppermute(last, axis, up)  53 us
    ppermute x14, waiting for transfers between devices, with_halo(): after = lax.ppermute(initial, axis, down)  40.5 us
    ppermute x14, starting transfers between devices, with_halo(): after = lax.ppermute(initial, axis, down)  31.3 us
    select_n x1, other arithmetic, on_device(): jnp.where(active, field + tendency(section_halo(field), speeds), 0.0)  14.1 us
    mul x1, other arithmetic, on_device(): sigma = ARCHIE * jnp.exp(advanced) * poro * poro * water * water  11.9 us
    reduce_sum x1, other arithmetic, on_device(): coarse = sigma.reshape(layers, coarse_x, 2, coarse_y, 2).sum(axis=(2, 4))  9.53 us
    all_gather x1, blocking collectives, serve_the_stops_all(): newest = lax.all_gather(base_x, axis_name)  6.51 us
    mul x1, local copies, waits for them, and re-layouts, on_device(): sigma = ARCHIE * jnp.exp(advanced) * poro * poro * water * water  6.36 us
  transfers between devices with their start and end apart: 28, of which 13 were waited for; matrix products, arithmetic and copies ran while one was open for 18% of the time, Pallas kernels for 0%

profile of v1, /device:TPU:70, one launch (start us, length us, event | category | flops | bytes accessed | tf_op | source)
XLA Modules:
  0.0 213.3 jit_solution(1642394528583420335)
XLA Ops:
  0.7 1.8 broadcast_select_fusion
  2.5 1.9 collective-permute-start
  4.4 3.6 %collective-permute-start.1 = (f32[1,64,256]{2,1,0:T(8,128)S(1)}, f32[1,64,256]{2,1,0:T(8,128)S(1)}, u32[]{:S(2)}, u32[]{:S(2)}) collective-permute-start(f32[1,64,256]{2,1,0:T(8,128)S(1)} %get-tuple-element.22), channel_id=1, source_target_pairs={{64,0},{128,64},{192,128},{65,1},{129,65},{193,129},{66,2},{130,66... | collective-permute-start | bytes 196616 | tf_op jit(solution)/shard_map/ppermute | solution.py:30
  8.2 4.7 %collective-permute-start.16 = (f32[1,8,1,128]{3,1,2,0:T(8,128)S(1)}, f32[1,8,1,128]{3,1,2,0:T(8,128)S(1)}, u32[]{:S(2)}, u32[]{:S(2)}) collective-permute-start(f32[1,8,1,128]{3,1,2,0:T(8,128)S(1)} %get-tuple-element.38), channel_id=1, source_target_pairs={{0,4},{4,8},{8,12},{12,16},{16,20},{20,24},{24,28},{28,32},{32,36}... | collective-permute-start | bytes 12296 | tf_op jit(solution)/shard_map/ppermute | solution.py:29
  12.9 2.7 %collective-permute-start.17 = (f32[1,8,1,128]{3,1,2,0:T(8,128)S(1)}, f32[1,8,1,128]{3,1,2,0:T(8,128)S(1)}, u32[]{:S(2)}, u32[]{:S(2)}) collective-permute-start(f32[1,8,1,128]{3,1,2,0:T(8,128)S(1)} %get-tuple-element.37), channel_id=1, source_target_pairs={{4,0},{8,4},{12,8},{16,12},{20,16},{24,20},{28,24},{32,28},{36,32}... | collective-permute-start | bytes 12296 | tf_op jit(solution)/shard_map/ppermute | solution.py:30
  15.6 1.8 fusion.129
  18.6 5.6 %collective-permute-start.2 = (f32[34,1,256]{2,1,0:T(1,128)S(1)}, f32[34,1,256]{2,1,0:T(1,128)S(1)}, u32[]{:S(2)}, u32[]{:S(2)}) collective-permute-start(f32[34,1,256]{2,1,0:T(1,128)S(1)} %get-tuple-element.17), channel_id=1, source_target_pairs={{0,4},{4,8},{8,12},{12,16},{16,20},{20,24},{24,28},{28,32},{32,36}... | collective-permute-start | bytes 104456 | tf_op jit(solution)/shard_map/ppermute | solution.py:29
  24.2 1.9 collective-permute-start.3
  26.1 6.3 %collective-permute-done.3 = f32[34,1,256]{2,1,0:T(1,128)S(1)} collective-permute-done((f32[34,1,256]{2,1,0:T(1,128)S(1)}, f32[34,1,256]{2,1,0:T(1,128)S(1)}, u32[]{:S(2)}, u32[]{:S(2)}) %collective-permute-start.3) | collective-permute-done | bytes 34848 | tf_op jit(solution)/shard_map/ppermute | solution.py:30
  32.8 1.9 fusion.118
  34.6 1.8 copy.23
  36.4 3.5 %collective-permute-start.4 = (f32[34,66,1]{1,2,0:T(1,128)S(1)}, f32[34,66,1]{1,2,0:T(1,128)S(1)}, u32[]{:S(2)}, u32[]{:S(2)}) collective-permute-start(f32[34,66,1]{1,2,0:T(1,128)S(1)} %copy.23), channel_id=1, source_target_pairs={{0,1},{1,2},{2,3},{4,5},{5,6},{6,7},{8,9},{9,10},{10,11},{12,13},{... | collective-permute-start | bytes 26936 | tf_op jit(solution)/shard_map/ppermute | solution.py:29
  41.7 5.4 %convert_element_type.64 = f32[3,1,32,64,256]{4,3,2,1,0:T(8,128)} convert(bf16[3,1,32,64,256]{4,3,2,1,0:T(8,128)(2,1)} %param.8) | non-fusion elementwise | flops 1572864 | bytes 9437184 | tf_op jit(solution)/shard_map/convert_element_type | solution.py:101
  48.7 1.6 copy.26
  50.3 14.1 %fusion.31 = f32[32,64,256]{2,1,0:T(8,128)S(1)} fusion(f32[32,64,256]{2,1,0:T(8,128)} %copy-done.1, f32[34,1,256]{2,1,0:T(1,128)S(1)} %collective-permute-done.3, f32[1,64,256]{2,1,0:T(8,128)S(1)} %collective-permute-done.1, f32[1,64,256]{2,1,0:T(8,128)S(1)} %collective-permute-done, f32[34,1,256]{2,1,0:T(1,128)S(1)} %collective-permute-done.2, ...), kind=kLoop, calls=%fused_computation.66 | loop fusion | flops 28311552 | bytes 10704417 | tf_op jit(solution)/shard_map/jit(_where)/select_n | solution.py:103
  64.5 1.9 collective-permute-start.6
  66.4 3.6 %collective-permute-start.7 = (f32[1,64,256]{2,1,0:T(8,128)S(1)}, f32[1,64,256]{2,1,0:T(8,128)S(1)}, u32[]{:S(2)}, u32[]{:S(2)}) collective-permute-start(f32[1,64,256]{2,1,0:T(8,128)S(1)} %get-tuple-element.20), channel_id=1, source_target_pairs={{64,0},{128,64},{192,128},{65,1},{129,65},{193,129},{66,2},{130,66... | collective-permute-start | bytes 196616 | tf_op jit(solution)/shard_map/ppermute | solution.py:30
  70.1 1.9 collective-permute-done.7
  72.0 4.8 %collective-permute-start.8 = (f32[34,1,256]{2,1,0:T(1,128)S(1)}, f32[34,1,256]{2,1,0:T(1,128)S(1)}, u32[]{:S(2)}, u32[]{:S(2)}) collective-permute-start(f32[34,1,256]{2,1,0:T(1,128)S(1)} %get-tuple-element.15), channel_id=1, source_target_pairs={{0,4},{4,8},{8,12},{12,16},{16,20},{20,24},{24,28},{28,32},{32,36}... | collective-permute-start | bytes 104456 | tf_op jit(solution)/shard_map/ppermute | solution.py:29
  76.8 2.5 %collective-permute-start.9 = (f32[34,1,256]{2,1,0:T(1,128)S(1)}, f32[34,1,256]{2,1,0:T(1,128)S(1)}, u32[]{:S(2)}, u32[]{:S(2)}) collective-permute-start(f32[34,1,256]{2,1,0:T(1,128)S(1)} %get-tuple-element.16), channel_id=1, source_target_pairs={{4,0},{8,4},{12,8},{16,12},{20,16},{24,20},{28,24},{32,28},{36,32}... | collective-permute-start | bytes 104456 | tf_op jit(solution)/shard_map/ppermute | solution.py:30
  79.5 6.8 %collective-permute-done.9 = f32[34,1,256]{2,1,0:T(1,128)S(1)} collective-permute-done((f32[34,1,256]{2,1,0:T(1,128)S(1)}, f32[34,1,256]{2,1,0:T(1,128)S(1)}, u32[]{:S(2)}, u32[]{:S(2)}) %collective-permute-start.9) | collective-permute-done | bytes 34848 | tf_op jit(solution)/shard_map/ppermute | solution.py:30
  86.6 1.8 fusion.117
  88.4 1.7 copy.27
  90.1 4.6 %collective-permute-start.10 = (f32[34,66,1]{1,2,0:T(1,128)S(1)}, f32[34,66,1]{1,2,0:T(1,128)S(1)}, u32[]{:S(2)}, u32[]{:S(2)}) collective-permute-start(f32[34,66,1]{1,2,0:T(1,128)S(1)} %copy.27), channel_id=1, source_target_pairs={{0,1},{1,2},{2,3},{4,5},{5,6},{6,7},{8,9},{9,10},{10,11},{12,13},{... | collective-permute-start | bytes 26936 | tf_op jit(solution)/shard_map/ppermute | solution.py:29
  94.7 1.7 copy.29
  99.5 2.6 %collective-permute-done.11 = f32[34,66,1]{1,2,0:T(1,128)S(1)} collective-permute-done((f32[34,66,1]{1,2,0:T(1,128)S(1)}, f32[34,66,1]{1,2,0:T(1,128)S(1)}, u32[]{:S(2)}, u32[]{:S(2)}) %collective-permute-start.11) | collective-permute-done | bytes 9008 | tf_op jit(solution)/shard_map/ppermute | solution.py:30
  103.7 11.9 %multiply_multiply_fusion = (f32[32,64,256]{2,1,0:T(8,128)}, f32[32,64,256]{2,1,0:T(8,128)}) fusion(bf16[1,32,64,256]{3,2,1,0:T(8,128)(2,1)} %param.10, bf16[1,32,64,256]{3,2,1,0:T(8,128)(2,1)} %param.9, f32[32,64,256]{2,1,0:T(8,128)S(1)} %fusion.31, f32[3,1,32,64,256]{4,3,2,1,0:T(8,128)} %convert_element_type.64, f32[34,66,1]{2,1,0:T(8,128)} %copy.30, ...), kind=kLoop, calls=%fused_computation | loop fusion | flops 33554432 | bytes 16996896 | tf_op jit(solution)/shard_map/mul | solution.py:108
  115.5 6.4 %copy.31 = f32[32,64,256]{0,2,1:T(8,128)} copy(f32[32,64,256]{2,1,0:T(8,128)} %get-tuple-element.9) | data formatting | bytes 4194304 | tf_op jit(solution)/shard_map/mul | solution.py:108
  121.9 9.5 %reduce_sum.18 = f32[32,32,128]{0,2,1:T(8,128)S(1)} reduce(f32[32,32,2,128,2]{0,4,3,2,1:T(2,128)} %bitcast.110, f32[]{:T(128)} %constant.8.clone.1), dimensions={2,4}, to_apply=%region_1.2 | reduce | flops 393216 | bytes 2621444 | tf_op jit(solution)/shard_map/reduce_sum | solution.py:111
  132.4 6.5 %all-gather = f32[32,32,128]{2,0,1:T(8,128)S(1)} all-gather(f32[8,32,128]{2,0,1:T(8,128)S(1)} %fusion.49), channel_id=2, replica_groups=mesh['grp'=4,'gx'=16,'gy'=4] {'grp'}, dimensions={0}, use_global_device_ids=true | all-gather | bytes 655360 | tf_op jit(solution)/shard_map/all_gather | solution.py:15
  139.0 5.4 %collective-permute-start.12 = (f32[8,1,128]{2,0,1:T(8,128)S(1)}, f32[8,1,128]{2,0,1:T(8,128)S(1)}, u32[]{:S(2)}, u32[]{:S(2)}) collective-permute-start(f32[8,1,128]{2,0,1:T(8,128)S(1)} %get-tuple-element.36), channel_id=1, source_target_pairs={{0,4},{4,8},{8,12},{12,16},{16,20},{20,24},{24,28},{28,32},{32,36}... | collective-permute-start | bytes 12296 | tf_op jit(solution)/shard_map/ppermute | solution.py:29
  144.4 1.9 collective-permute-start.13
  146.4 3.5 %collective-permute-start.18 = (f32[1,8,34,1]{3,1,2,0:T(8,128)S(1)}, f32[1,8,34,1]{3,1,2,0:T(8,128)S(1)}, u32[]{:S(2)}, u32[]{:S(2)}) collective-permute-start(f32[1,8,34,1]{3,1,2,0:T(8,128)S(1)} %get-tuple-element.29), channel_id=1, source_target_pairs={{0,1},{1,2},{2,3},{4,5},{5,6},{6,7},{8,9},{9,10},{10,11},{12,13},{... | collective-permute-start | bytes 3272 | tf_op jit(solution)/shard_map/ppermute | solution.py:29
  152.4 3.5 %collective-permute-start.14 = (f32[8,34,1]{2,0,1:T(8,128)S(1)}, f32[8,34,1]{2,0,1:T(8,128)S(1)}, u32[]{:S(2)}, u32[]{:S(2)}) collective-permute-start(f32[8,34,1]{2,0,1:T(8,128)S(1)} %get-tuple-element.28), channel_id=1, source_target_pairs={{0,1},{1,2},{2,3},{4,5},{5,6},{6,7},{8,9},{9,10},{10,11},{12,13},{... | collective-permute-start | bytes 3272 | tf_op jit(solution)/shard_map/ppermute | solution.py:29
  158.5 4.4 %collective-permute-done.15 = f32[8,34,1]{2,0,1:T(8,128)S(1)} collective-permute-done((f32[8,34,1]{2,0,1:T(8,128)S(1)}, f32[8,34,1]{2,0,1:T(8,128)S(1)}, u32[]{:S(2)}, u32[]{:S(2)}) %collective-permute-start.15) | collective-permute-done | bytes 1120 | tf_op jit(solution)/shard_map/ppermute | solution.py:30
  163.2 1.7 fusion.86
  164.9 6.3 %collective-permute-start.20 = (f32[1,8,1,128]{3,1,2,0:T(8,128)S(1)}, f32[1,8,1,128]{3,1,2,0:T(8,128)S(1)}, u32[]{:S(2)}, u32[]{:S(2)}) collective-permute-start(f32[1,8,1,128]{3,1,2,0:T(8,128)S(1)} %get-tuple-element.33), channel_id=1, source_target_pairs={{0,4},{4,8},{8,12},{12,16},{16,20},{20,24},{24,28},{28,32},{32,36}... | collective-permute-start | bytes 12296 | tf_op jit(solution)/shard_map/ppermute | solution.py:29
  171.3 1.9 collective-permute-start.21
  173.2 6.0 %collective-permute-done.21 = f32[1,8,1,128]{3,1,2,0:T(8,128)S(1)} collective-permute-done((f32[1,8,1,128]{3,1,2,0:T(8,128)S(1)}, f32[1,8,1,128]{3,1,2,0:T(8,128)S(1)}, u32[]{:S(2)}, u32[]{:S(2)}) %collective-permute-start.21) | collective-permute-done | bytes 4128 | tf_op jit(solution)/shard_map/ppermute | solution.py:30
  179.3 3.2 %collective-permute-start.22 = (f32[1,8,34,1]{3,1,2,0:T(8,128)S(1)}, f32[1,8,34,1]{3,1,2,0:T(8,128)S(1)}, u32[]{:S(2)}, u32[]{:S(2)}) collective-permute-start(f32[1,8,34,1]{3,1,2,0:T(8,128)S(1)} %get-tuple-element.25), channel_id=1, source_target_pairs={{0,1},{1,2},{2,3},{4,5},{5,6},{6,7},{8,9},{9,10},{10,11},{12,13},{... | collective-permute-start | bytes 3272 | tf_op jit(solution)/shard_map/ppermute | solution.py:29
  185.0 4.4 %collective-permute-done.23 = f32[1,8,34,1]{3,1,2,0:T(8,128)S(1)} collective-permute-done((f32[1,8,34,1]{3,1,2,0:T(8,128)S(1)}, f32[1,8,34,1]{3,1,2,0:T(8,128)S(1)}, u32[]{:S(2)}, u32[]{:S(2)}) %collective-permute-start.23) | collective-permute-done | bytes 1120 | tf_op jit(solution)/shard_map/ppermute | solution.py:30
  189.7 1.7 fusion.72
  191.4 2.2 %collective-permute-start.24 = (f32[1,8,1,128]{3,1,2,0:T(8,128)S(1)}, f32[1,8,1,128]{3,1,2,0:T(8,128)S(1)}, u32[]{:S(2)}, u32[]{:S(2)}) collective-permute-start(f32[1,8,1,128]{3,1,2,0:T(8,128)S(1)} %get-tuple-element.31), channel_id=1, source_target_pairs={{0,4},{4,8},{8,12},{12,16},{16,20},{20,24},{24,28},{28,32},{32,36}... | collective-permute-start | bytes 12296 | tf_op jit(solution)/shard_map/ppermute | solution.py:29
  193.7 5.1 %collective-permute-start.25 = (f32[1,8,1,128]{3,1,2,0:T(8,128)S(1)}, f32[1,8,1,128]{3,1,2,0:T(8,128)S(1)}, u32[]{:S(2)}, u32[]{:S(2)}) collective-permute-start(f32[1,8,1,128]{3,1,2,0:T(8,128)S(1)} %get-tuple-element.32), channel_id=1, source_target_pairs={{4,0},{8,4},{12,8},{16,12},{20,16},{24,20},{28,24},{32,28},{36,32}... | collective-permute-start | bytes 12296 | tf_op jit(solution)/shard_map/ppermute | solution.py:30
  198.8 2.8 %collective-permute-done.25 = f32[1,8,1,128]{3,1,2,0:T(8,128)S(1)} collective-permute-done((f32[1,8,1,128]{3,1,2,0:T(8,128)S(1)}, f32[1,8,1,128]{3,1,2,0:T(8,128)S(1)}, u32[]{:S(2)}, u32[]{:S(2)}) %collective-permute-start.25) | collective-permute-done | bytes 4128 | tf_op jit(solution)/shard_map/ppermute | solution.py:30
  201.7 1.9 collective-permute-start.26
  206.2 4.4 %collective-permute-done.27 = f32[1,8,34,1]{3,1,2,0:T(8,128)S(1)} collective-permute-done((f32[1,8,34,1]{3,1,2,0:T(8,128)S(1)}, f32[1,8,34,1]{3,1,2,0:T(8,128)S(1)}, u32[]{:S(2)}, u32[]{:S(2)}) %collective-permute-start.27) | collective-permute-done | bytes 1120 | tf_op jit(solution)/shard_map/ppermute | solution.py:30
  210.9 1.7 fusion.58
  (80 shorter events, 23.1 us)
Async XLA Ops:
  0.6 7.4 %copy-start = (f32[4,8,32,128]{3,2,1,0:T(8,128)S(1)}, f32[4,8,32,128]{3,2,1,0:T(8,128)}, u32[]{:S(2)}) copy-start(f32[4,8,32,128]{3,2,1,0:T(8,128)} %param.13) | copy-start | bytes 1572868
  2.5 16.1 %collective-permute-start = (f32[1,64,256]{2,1,0:T(8,128)S(1)}, f32[1,64,256]{2,1,0:T(8,128)S(1)}, u32[]{:S(2)}, u32[]{:S(2)}) collective-permute-start(f32[1,64,256]{2,1,0:T(8,128)S(1)} %get-tuple-element.21), channel_id=1, source_target_pairs={{0,64},{64,128},{128,192},{1,65},{65,129},{129,193},{2,66},{66,130... | collective-permute-start | bytes 196616 | tf_op jit(solution)/shard_map/ppermute | solution.py:29
  4.4 14.2 %collective-permute-start.1 = (f32[1,64,256]{2,1,0:T(8,128)S(1)}, f32[1,64,256]{2,1,0:T(8,128)S(1)}, u32[]{:S(2)}, u32[]{:S(2)}) collective-permute-start(f32[1,64,256]{2,1,0:T(8,128)S(1)} %get-tuple-element.22), channel_id=1, source_target_pairs={{64,0},{128,64},{192,128},{65,1},{129,65},{193,129},{66,2},{130,66... | collective-permute-start | bytes 196616 | tf_op jit(solution)/shard_map/ppermute | solution.py:30
  8.2 61.9 %collective-permute-start.16 = (f32[1,8,1,128]{3,1,2,0:T(8,128)S(1)}, f32[1,8,1,128]{3,1,2,0:T(8,128)S(1)}, u32[]{:S(2)}, u32[]{:S(2)}) collective-permute-start(f32[1,8,1,128]{3,1,2,0:T(8,128)S(1)} %get-tuple-element.38), channel_id=1, source_target_pairs={{0,4},{4,8},{8,12},{12,16},{16,20},{20,24},{24,28},{28,32},{32,36}... | collective-permute-start | bytes 12296 | tf_op jit(solution)/shard_map/ppermute | solution.py:29
  12.9 4.5 %copy-start.4 = (s32[8]{0:T(128)S(1)}, s32[8]{0:T(128)}, u32[]{:S(2)}) copy-start(s32[8]{0:T(128)} %param.11) | copy-start | bytes 100
  12.9 4.7 %copy-start.3 = (s32[4,2]{0,1:T(2,128)S(1)}, s32[4,2]{0,1:T(2,128)}, u32[]{:S(2)}) copy-start(s32[4,2]{0,1:T(2,128)} %param.12) | copy-start | bytes 100
  12.9 85.1 %collective-permute-start.17 = (f32[1,8,1,128]{3,1,2,0:T(8,128)S(1)}, f32[1,8,1,128]{3,1,2,0:T(8,128)S(1)}, u32[]{:S(2)}, u32[]{:S(2)}) collective-permute-start(f32[1,8,1,128]{3,1,2,0:T(8,128)S(1)} %get-tuple-element.37), channel_id=1, source_target_pairs={{4,0},{8,4},{12,8},{16,12},{20,16},{24,20},{28,24},{32,28},{36,32}... | collective-permute-start | bytes 12296 | tf_op jit(solution)/shard_map/ppermute | solution.py:30
  17.3 15.4 %copy-start.1 = (f32[32,64,256]{2,1,0:T(8,128)}, f32[32,64,256]{2,1,0:T(8,128)S(1)}, u32[]{:S(2)}) copy-start(f32[32,64,256]{2,1,0:T(8,128)S(1)} %fusion.129) | copy-start | bytes 6291460
  18.6 7.5 %collective-permute-start.2 = (f32[34,1,256]{2,1,0:T(1,128)S(1)}, f32[34,1,256]{2,1,0:T(1,128)S(1)}, u32[]{:S(2)}, u32[]{:S(2)}) collective-permute-start(f32[34,1,256]{2,1,0:T(1,128)S(1)} %get-tuple-element.17), channel_id=1, source_target_pairs={{0,4},{4,8},{8,12},{12,16},{16,20},{20,24},{24,28},{28,32},{32,36}... | collective-permute-start | bytes 104456 | tf_op jit(solution)/shard_map/ppermute | solution.py:29
  24.2 8.2 %collective-permute-start.3 = (f32[34,1,256]{2,1,0:T(1,128)S(1)}, f32[34,1,256]{2,1,0:T(1,128)S(1)}, u32[]{:S(2)}, u32[]{:S(2)}) collective-permute-start(f32[34,1,256]{2,1,0:T(1,128)S(1)} %get-tuple-element.18), channel_id=1, source_target_pairs={{4,0},{8,4},{12,8},{16,12},{20,16},{24,20},{28,24},{32,28},{36,32}... | collective-permute-start | bytes 104456 | tf_op jit(solution)/shard_map/ppermute | solution.py:30
  34.6 5.3 %copy-start.2 = (f32[34,66,1]{2,1,0:T(8,128)S(1)}, f32[34,66,1]{2,1,0:T(8,128)}, u32[]{:S(2)}) copy-start(f32[34,66,1]{2,1,0:T(8,128)} %get-tuple-element.13) | copy-start | bytes 26932
  36.4 10.7 %collective-permute-start.4 = (f32[34,66,1]{1,2,0:T(1,128)S(1)}, f32[34,66,1]{1,2,0:T(1,128)S(1)}, u32[]{:S(2)}, u32[]{:S(2)}) collective-permute-start(f32[34,66,1]{1,2,0:T(1,128)S(1)} %copy.23), channel_id=1, source_target_pairs={{0,1},{1,2},{2,3},{4,5},{5,6},{6,7},{8,9},{9,10},{10,11},{12,13},{... | collective-permute-start | bytes 26936 | tf_op jit(solution)/shard_map/ppermute | solution.py:29
  40.4 8.3 %collective-permute-start.5 = (f32[34,66,1]{1,2,0:T(1,128)S(1)}, f32[34,66,1]{1,2,0:T(1,128)S(1)}, u32[]{:S(2)}, u32[]{:S(2)}) collective-permute-start(f32[34,66,1]{1,2,0:T(1,128)S(1)} %copy.25), channel_id=1, source_target_pairs={{1,0},{2,1},{3,2},{5,4},{6,5},{7,6},{9,8},{10,9},{11,10},{13,12},{... | collective-permute-start | bytes 26936 | tf_op jit(solution)/shard_map/ppermute | solution.py:30
  64.5 5.6 %collective-permute-start.6 = (f32[1,64,256]{2,1,0:T(8,128)S(1)}, f32[1,64,256]{2,1,0:T(8,128)S(1)}, u32[]{:S(2)}, u32[]{:S(2)}) collective-permute-start(f32[1,64,256]{2,1,0:T(8,128)S(1)} %get-tuple-element.19), channel_id=1, source_target_pairs={{0,64},{64,128},{128,192},{1,65},{65,129},{129,193},{2,66},{66,130... | collective-permute-start | bytes 196616 | tf_op jit(solution)/shard_map/ppermute | solution.py:29
  66.4 5.5 %collective-permute-start.7 = (f32[1,64,256]{2,1,0:T(8,128)S(1)}, f32[1,64,256]{2,1,0:T(8,128)S(1)}, u32[]{:S(2)}, u32[]{:S(2)}) collective-permute-start(f32[1,64,256]{2,1,0:T(8,128)S(1)} %get-tuple-element.20), channel_id=1, source_target_pairs={{64,0},{128,64},{192,128},{65,1},{129,65},{193,129},{66,2},{130,66... | collective-permute-start | bytes 196616 | tf_op jit(solution)/shard_map/ppermute | solution.py:30
  72.0 7.5 %collective-permute-start.8 = (f32[34,1,256]{2,1,0:T(1,128)S(1)}, f32[34,1,256]{2,1,0:T(1,128)S(1)}, u32[]{:S(2)}, u32[]{:S(2)}) collective-permute-start(f32[34,1,256]{2,1,0:T(1,128)S(1)} %get-tuple-element.15), channel_id=1, source_target_pairs={{0,4},{4,8},{8,12},{12,16},{16,20},{20,24},{24,28},{28,32},{32,36}... | collective-permute-start | bytes 104456 | tf_op jit(solution)/shard_map/ppermute | solution.py:29
  76.8 9.4 %collective-permute-start.9 = (f32[34,1,256]{2,1,0:T(1,128)S(1)}, f32[34,1,256]{2,1,0:T(1,128)S(1)}, u32[]{:S(2)}, u32[]{:S(2)}) collective-permute-start(f32[34,1,256]{2,1,0:T(1,128)S(1)} %get-tuple-element.16), channel_id=1, source_target_pairs={{4,0},{8,4},{12,8},{16,12},{20,16},{24,20},{28,24},{32,28},{36,32}... | collective-permute-start | bytes 104456 | tf_op jit(solution)/shard_map/ppermute | solution.py:30
  90.1 7.8 %collective-permute-start.10 = (f32[34,66,1]{1,2,0:T(1,128)S(1)}, f32[34,66,1]{1,2,0:T(1,128)S(1)}, u32[]{:S(2)}, u32[]{:S(2)}) collective-permute-start(f32[34,66,1]{1,2,0:T(1,128)S(1)} %copy.27), channel_id=1, source_target_pairs={{0,1},{1,2},{2,3},{4,5},{5,6},{6,7},{8,9},{9,10},{10,11},{12,13},{... | collective-permute-start | bytes 26936 | tf_op jit(solution)/shard_map/ppermute | solution.py:29
  96.5 5.7 %collective-permute-start.11 = (f32[34,66,1]{1,2,0:T(1,128)S(1)}, f32[34,66,1]{1,2,0:T(1,128)S(1)}, u32[]{:S(2)}, u32[]{:S(2)}) collective-permute-start(f32[34,66,1]{1,2,0:T(1,128)S(1)} %copy.29), channel_id=1, source_target_pairs={{1,0},{2,1},{3,2},{5,4},{6,5},{7,6},{9,8},{10,9},{11,10},{13,12},{... | collective-permute-start | bytes 26936 | tf_op jit(solution)/shard_map/ppermute | solution.py:30
  139.0 12.3 %collective-permute-start.12 = (f32[8,1,128]{2,0,1:T(8,128)S(1)}, f32[8,1,128]{2,0,1:T(8,128)S(1)}, u32[]{:S(2)}, u32[]{:S(2)}) collective-permute-start(f32[8,1,128]{2,0,1:T(8,128)S(1)} %get-tuple-element.36), channel_id=1, source_target_pairs={{0,4},{4,8},{8,12},{12,16},{16,20},{20,24},{24,28},{28,32},{32,36}... | collective-permute-start | bytes 12296 | tf_op jit(solution)/shard_map/ppermute | solution.py:29
  144.4 7.9 %collective-permute-start.13 = (f32[8,1,128]{2,0,1:T(8,128)S(1)}, f32[8,1,128]{2,0,1:T(8,128)S(1)}, u32[]{:S(2)}, u32[]{:S(2)}) collective-permute-start(f32[8,1,128]{2,0,1:T(8,128)S(1)} %get-tuple-element.35), channel_id=1, source_target_pairs={{4,0},{8,4},{12,8},{16,12},{20,16},{24,20},{28,24},{32,28},{36,32}... | collective-permute-start | bytes 12296 | tf_op jit(solution)/shard_map/ppermute | solution.py:30
  146.4 10.8 %collective-permute-start.18 = (f32[1,8,34,1]{3,1,2,0:T(8,128)S(1)}, f32[1,8,34,1]{3,1,2,0:T(8,128)S(1)}, u32[]{:S(2)}, u32[]{:S(2)}) collective-permute-start(f32[1,8,34,1]{3,1,2,0:T(8,128)S(1)} %get-tuple-element.29), channel_id=1, source_target_pairs={{0,1},{1,2},{2,3},{4,5},{5,6},{6,7},{8,9},{9,10},{10,11},{12,13},{... | collective-permute-start | bytes 3272 | tf_op jit(solution)/shard_map/ppermute | solution.py:29
  149.9 7.3 %collective-permute-start.19 = (f32[1,8,34,1]{3,1,2,0:T(8,128)S(1)}, f32[1,8,34,1]{3,1,2,0:T(8,128)S(1)}, u32[]{:S(2)}, u32[]{:S(2)}) collective-permute-start(f32[1,8,34,1]{3,1,2,0:T(8,128)S(1)} %get-tuple-element.30), channel_id=1, source_target_pairs={{1,0},{2,1},{3,2},{5,4},{6,5},{7,6},{9,8},{10,9},{11,10},{13,12},{... | collective-permute-start | bytes 3272 | tf_op jit(solution)/shard_map/ppermute | solution.py:30
  152.4 6.1 %collective-permute-start.14 = (f32[8,34,1]{2,0,1:T(8,128)S(1)}, f32[8,34,1]{2,0,1:T(8,128)S(1)}, u32[]{:S(2)}, u32[]{:S(2)}) collective-permute-start(f32[8,34,1]{2,0,1:T(8,128)S(1)} %get-tuple-element.28), channel_id=1, source_target_pairs={{0,1},{1,2},{2,3},{4,5},{5,6},{6,7},{8,9},{9,10},{10,11},{12,13},{... | collective-permute-start | bytes 3272 | tf_op jit(solution)/shard_map/ppermute | solution.py:29
  155.9 6.9 %collective-permute-start.15 = (f32[8,34,1]{2,0,1:T(8,128)S(1)}, f32[8,34,1]{2,0,1:T(8,128)S(1)}, u32[]{:S(2)}, u32[]{:S(2)}) collective-permute-start(f32[8,34,1]{2,0,1:T(8,128)S(1)} %get-tuple-element.27), channel_id=1, source_target_pairs={{1,0},{2,1},{3,2},{5,4},{6,5},{7,6},{9,8},{10,9},{11,10},{13,12},{... | collective-permute-start | bytes 3272 | tf_op jit(solution)/shard_map/ppermute | solution.py:30
  164.9 8.3 %collective-permute-start.20 = (f32[1,8,1,128]{3,1,2,0:T(8,128)S(1)}, f32[1,8,1,128]{3,1,2,0:T(8,128)S(1)}, u32[]{:S(2)}, u32[]{:S(2)}) collective-permute-start(f32[1,8,1,128]{3,1,2,0:T(8,128)S(1)} %get-tuple-element.33), channel_id=1, source_target_pairs={{0,4},{4,8},{8,12},{12,16},{16,20},{20,24},{24,28},{28,32},{32,36}... | collective-permute-start | bytes 12296 | tf_op jit(solution)/shard_map/ppermute | solution.py:29
  171.3 7.9 %collective-permute-start.21 = (f32[1,8,1,128]{3,1,2,0:T(8,128)S(1)}, f32[1,8,1,128]{3,1,2,0:T(8,128)S(1)}, u32[]{:S(2)}, u32[]{:S(2)}) collective-permute-start(f32[1,8,1,128]{3,1,2,0:T(8,128)S(1)} %get-tuple-element.34), channel_id=1, source_target_pairs={{4,0},{8,4},{12,8},{16,12},{20,16},{24,20},{28,24},{32,28},{36,32}... | collective-permute-start | bytes 12296 | tf_op jit(solution)/shard_map/ppermute | solution.py:30
  179.3 5.8 %collective-permute-start.22 = (f32[1,8,34,1]{3,1,2,0:T(8,128)S(1)}, f32[1,8,34,1]{3,1,2,0:T(8,128)S(1)}, u32[]{:S(2)}, u32[]{:S(2)}) collective-permute-start(f32[1,8,34,1]{3,1,2,0:T(8,128)S(1)} %get-tuple-element.25), channel_id=1, source_target_pairs={{0,1},{1,2},{2,3},{4,5},{5,6},{6,7},{8,9},{9,10},{10,11},{12,13},{... | collective-permute-start | bytes 3272 | tf_op jit(solution)/shard_map/ppermute | solution.py:29
  182.5 6.9 %collective-permute-start.23 = (f32[1,8,34,1]{3,1,2,0:T(8,128)S(1)}, f32[1,8,34,1]{3,1,2,0:T(8,128)S(1)}, u32[]{:S(2)}, u32[]{:S(2)}) collective-permute-start(f32[1,8,34,1]{3,1,2,0:T(8,128)S(1)} %get-tuple-element.26), channel_id=1, source_target_pairs={{1,0},{2,1},{3,2},{5,4},{6,5},{7,6},{9,8},{10,9},{11,10},{13,12},{... | collective-permute-start | bytes 3272 | tf_op jit(solution)/shard_map/ppermute | solution.py:30
  191.4 7.4 %collective-permute-start.24 = (f32[1,8,1,128]{3,1,2,0:T(8,128)S(1)}, f32[1,8,1,128]{3,1,2,0:T(8,128)S(1)}, u32[]{:S(2)}, u32[]{:S(2)}) collective-permute-start(f32[1,8,1,128]{3,1,2,0:T(8,128)S(1)} %get-tuple-element.31), channel_id=1, source_target_pairs={{0,4},{4,8},{8,12},{12,16},{16,20},{20,24},{24,28},{28,32},{32,36}... | collective-permute-start | bytes 12296 | tf_op jit(solution)/shard_map/ppermute | solution.py:29
  193.7 7.9 %collective-permute-start.25 = (f32[1,8,1,128]{3,1,2,0:T(8,128)S(1)}, f32[1,8,1,128]{3,1,2,0:T(8,128)S(1)}, u32[]{:S(2)}, u32[]{:S(2)}) collective-permute-start(f32[1,8,1,128]{3,1,2,0:T(8,128)S(1)} %get-tuple-element.32), channel_id=1, source_target_pairs={{4,0},{8,4},{12,8},{16,12},{20,16},{24,20},{28,24},{32,28},{36,32}... | collective-permute-start | bytes 12296 | tf_op jit(solution)/shard_map/ppermute | solution.py:30
  201.7 4.5 %collective-permute-start.26 = (f32[1,8,34,1]{3,1,2,0:T(8,128)S(1)}, f32[1,8,34,1]{3,1,2,0:T(8,128)S(1)}, u32[]{:S(2)}, u32[]{:S(2)}) collective-permute-start(f32[1,8,34,1]{3,1,2,0:T(8,128)S(1)} %get-tuple-element.23), channel_id=1, source_target_pairs={{0,1},{1,2},{2,3},{4,5},{5,6},{6,7},{8,9},{9,10},{10,11},{12,13},{... | collective-permute-start | bytes 3272 | tf_op jit(solution)/shard_map/ppermute | solution.py:29
  203.7 6.9 %collective-permute-start.27 = (f32[1,8,34,1]{3,1,2,0:T(8,128)S(1)}, f32[1,8,34,1]{3,1,2,0:T(8,128)S(1)}, u32[]{:S(2)}, u32[]{:S(2)}) collective-permute-start(f32[1,8,34,1]{3,1,2,0:T(8,128)S(1)} %get-tuple-element.24), channel_id=1, source_target_pairs={{1,0},{2,1},{3,2},{5,4},{6,5},{7,6},{9,8},{10,9},{11,10},{13,12},{... | collective-permute-start | bytes 3272 | tf_op jit(solution)/shard_map/ppermute | solution.py:30
